TPU v7x, 256 devices: a whole 4x4x8 slice. The times are simulated.
256 devices in a mesh: pipe: 4 (over x), expert: 16 (over z, core), dp: 4 (over y).
Axes of the slice: x: 4, y: 4, z: 8, core: 2. Of those that a mesh axis runs over, the one named last changes fastest.
Arguments:
- inputs: bfloat16 [4, 8192, 4096], P('pipe', ('expert', 'dp')), may hold values from -6 to 6
- routes: int32 [4, 8192, 1], P('pipe', ('expert', 'dp')), may hold values from 0 to 15; in each aligned block of 128 rows (0 to 127, 128 to 255, ..., all dimensions but the last counted through in order) at most 10 rows name the same one
- router_scores: float32 [4, 8192, 8], P('pipe', ('expert', 'dp')), may hold values from -2 to 2
- cotangent: bfloat16 [4, 8192, 4096], P('pipe', ('expert', 'dp')), may hold values from -6 to 6
- w_gate: bfloat16 [4, 16, 768, 4096], P('pipe', 'expert', 'dp'), may hold values from -0.09375 to 0.09375
- w_up: bfloat16 [4, 16, 768, 4096], P('pipe', 'expert', 'dp'), may hold values from -0.09375 to 0.09375
- w_down: bfloat16 [4, 16, 768, 4096], P('pipe', 'expert', 'dp'), may hold values from -0.21875 to 0.21875
Outputs:
- score_grad: float32 [4, 8192, 8], P('pipe', ('expert', 'dp'))
- grad_prev: bfloat16 [4, 8192, 4096], P('pipe', ('expert', 'dp'))
- grad_gate: bfloat16 [4, 16, 768, 4096], P('pipe', 'expert', 'dp')
- grad_up: bfloat16 [4, 16, 768, 4096], P('pipe', 'expert', 'dp')
- grad_down: bfloat16 [4, 16, 768, 4096], P('pipe', 'expert', 'dp')
Inputs may be any that keep to these rules, and one draw needn't show every extreme that they name: `routes`: among the 128 tokens of one device in one section (one block) no expert is named more than 10 times, and in every draw some block names some expert exactly 10 times. Every expert is named by some token.
All inputs are finite; a program needn't handle non-finite values.
Results may differ from a plain program's by a relative error of at most 0.02.
Values may be sent and summed in bfloat16 or wider, within the bound.
No kernel may reach another device: no remote copies, remote signals or barrier semaphores. Data moves between devices by JAX's collectives and lax.ppermute only.
A program may use at most 128 MiB of HBM per device.

v0:
```python
import jax
import jax.numpy as jnp
from jax import lax
from jax.sharding import PartitionSpec as P


def from_behind(shard, axis, by):
    length = lax.axis_size(axis)
    pairs = [(i, i + by) for i in range(length) if 0 <= i + by < length]
    return lax.ppermute(shard, axis, pairs)


def route_tables(route_col, score_rows, experts, capacity):
    expert_ids = jnp.arange(experts, dtype=jnp.int32)
    onehot = (route_col[:, None] == expert_ids).astype(jnp.int32)
    earlier = jnp.cumsum(onehot, axis=0) - onehot
    slot = jnp.sum(onehot * earlier, axis=1)
    position = route_col * capacity + slot
    raised = jnp.exp(score_rows)
    weights = raised / jnp.sum(raised, axis=1, keepdims=True)
    gate = lax.optimization_barrier(weights[:, 0].astype(jnp.bfloat16)).astype(jnp.float32)
    table = position[:, None] == jnp.arange(experts * capacity, dtype=jnp.int32)
    return (weights, gate, table)


def per_device(inputs, routes, router_scores, cotangent, w_gate, w_up, w_down):
    tokens_in = inputs[0]
    upstream = cotangent[0]
    route_col = routes[0][:, 0]
    score_rows = router_scores[0]
    gate_mat = w_gate[0, 0]
    up_mat = w_up[0, 0]
    down_mat = w_down[0, 0]
    experts = lax.axis_size("expert")
    groups = lax.axis_size("dp")
    token_count, model_width = tokens_in.shape
    capacity = max(2, token_count * 5 // (4 * experts))
    weights, gate, table = route_tables(route_col, score_rows, experts, capacity)
    table_half = table.astype(jnp.bfloat16)
    token_contract = (((0,), (0,)), ((), ()))
    feature_contract = (((1,), (1,)), ((), ()))
    local_x = lax.dot_general(
        table_half, tokens_in, token_contract, preferred_element_type=jnp.float32
    )
    local_x = local_x.astype(jnp.bfloat16).reshape(experts, capacity, model_width)
    local_up = lax.dot_general(
        table_half, upstream, token_contract, preferred_element_type=jnp.float32
    )
    local_up = local_up.astype(jnp.bfloat16).reshape(experts, capacity, model_width)
    local_gate = jnp.sum(jnp.where(table, gate[:, None], jnp.float32(0.0)), axis=0)
    local_gate = local_gate.astype(jnp.bfloat16).reshape(experts, capacity)
    x_e = lax.all_to_all(local_x, "expert", 0, 0, tiled=True)
    up_e = lax.all_to_all(local_up, "expert", 0, 0, tiled=True)
    gate_e = lax.all_to_all(local_gate, "expert", 0, 0, tiled=True)
    rows_x = lax.all_gather(x_e, "dp", axis=0, tiled=True).reshape(-1, model_width)
    rows_up = lax.all_gather(up_e, "dp", axis=0, tiled=True).reshape(-1, model_width)
    rows_gate = lax.all_gather(gate_e, "dp", axis=0, tiled=True).reshape(-1)
    rows_grad = (rows_gate.astype(jnp.float32)[:, None] * rows_up.astype(jnp.float32)).astype(
        jnp.bfloat16
    )
    gate_pre = lax.dot_general(
        rows_x, gate_mat, feature_contract, preferred_element_type=jnp.float32
    )
    up_pre = lax.dot_general(rows_x, up_mat, feature_contract, preferred_element_type=jnp.float32)
    gate_sig = jax.nn.sigmoid(gate_pre)
    activated = (gate_pre * gate_sig * up_pre).astype(jnp.bfloat16)
    partial_out = jnp.dot(activated, down_mat, preferred_element_type=jnp.float32)
    row_score = jnp.sum(partial_out * rows_up.astype(jnp.float32), axis=1)
    row_score = lax.psum_scatter(
        row_score.reshape(groups, experts, capacity), "dp", scatter_dimension=0, tiled=True
    ).reshape(experts, capacity)
    slot_score = lax.all_to_all(row_score, "expert", 0, 0, tiled=True).reshape(-1)
    gate_grad = jnp.sum(jnp.where(table, slot_score[None, :], jnp.float32(0.0)), axis=1)
    is_first = (jnp.arange(score_rows.shape[1]) == 0).astype(jnp.float32)
    score_grad = gate_grad[:, None] * weights[:, 0:1] * (is_first - weights)
    hidden_grad = lax.dot_general(
        rows_grad, down_mat, feature_contract, preferred_element_type=jnp.float32
    )
    pre_gate = (hidden_grad * up_pre * gate_sig * (1.0 + gate_pre * (1.0 - gate_sig))).astype(
        jnp.bfloat16
    )
    pre_up = (hidden_grad * gate_pre * gate_sig).astype(jnp.bfloat16)
    grad_down = lax.dot_general(
        activated, rows_grad, token_contract, preferred_element_type=jnp.float32
    ).astype(jnp.bfloat16)
    grad_gate = lax.dot_general(
        pre_gate, rows_x, token_contract, preferred_element_type=jnp.float32
    ).astype(jnp.bfloat16)
    grad_up = lax.dot_general(
        pre_up, rows_x, token_contract, preferred_element_type=jnp.float32
    ).astype(jnp.bfloat16)
    partial_in = jnp.dot(pre_gate, gate_mat, preferred_element_type=jnp.float32)
    partial_in = partial_in + jnp.dot(pre_up, up_mat, preferred_element_type=jnp.float32)
    outgoing = partial_in.astype(jnp.bfloat16).reshape(groups, experts, capacity, model_width)
    summed = lax.psum_scatter(outgoing, "dp", scatter_dimension=0, tiled=True)
    summed = summed.reshape(experts, capacity, model_width)
    flat_in = lax.all_to_all(summed, "expert", 0, 0, tiled=True).reshape(-1, model_width)
    input_grad = jnp.dot(table_half, flat_in, preferred_element_type=jnp.float32).astype(
        jnp.bfloat16
    )
    handed = from_behind(input_grad, "pipe", -1)
    return (
        score_grad[None],
        handed[None],
        grad_gate[None, None],
        grad_up[None, None],
        grad_down[None, None],
    )


def solution(mesh):
    in_specs = (
        P("pipe", ("expert", "dp"), None),
        P("pipe", ("expert", "dp"), None),
        P("pipe", ("expert", "dp"), None),
        P("pipe", ("expert", "dp"), None),
        P("pipe", "expert", "dp", None),
        P("pipe", "expert", "dp", None),
        P("pipe", "expert", "dp", None),
    )
    out_specs = (
        P("pipe", ("expert", "dp"), None),
        P("pipe", ("expert", "dp"), None),
        P("pipe", "expert", "dp", None),
        P("pipe", "expert", "dp", None),
        P("pipe", "expert", "dp", None),
    )
    return jax.shard_map(
        per_device, mesh=mesh, in_specs=in_specs, out_specs=out_specs, check_vma=False
    )
```

profile of v0, /device:TPU:1, one launch (start us, length us, event | category | flops | bytes accessed | tf_op | source)
XLA Modules:
  0.0 496.6 jit_solution(5466417958805610884)
XLA Ops:
  13.1 61.0 %all_to_all.33 = bf16[16,10,4096]{2,1,0:T(8,128)(2,1)S(1)} all-to-all(bf16[16,10,4096]{2,1,0:T(8,128)(2,1)} %reshape.106), channel_id=1, replica_groups=mesh['pipe'=4,'expert'=16,'dp'=4] {'expert'}, dimensions={0} | all-to-all | bytes 2621440 | tf_op jit(solution)/shard_map/all_to_all | solution.py:53
  79.2 53.9 %all_to_all.34 = bf16[16,10,4096]{2,1,0:T(8,128)(2,1)S(1)} all-to-all(bf16[16,10,4096]{2,1,0:T(8,128)(2,1)} %reshape.104), channel_id=1, replica_groups=mesh['pipe'=4,'expert'=16,'dp'=4] {'expert'}, dimensions={0} | all-to-all | bytes 2621440 | tf_op jit(solution)/shard_map/all_to_all | solution.py:52
  135.2 12.2 %copy.39 = f32[64,10,4096]{2,1,0:T(8,128)} copy(bf16[64,10,4096]{2,0,1:T(8,128)(2,1)} %all-gather.6.cloned.1.call-done) | data formatting | bytes 15728640 | tf_op jit(solution)/shard_map/convert_element_type | solution.py:68
  147.4 12.4 %reshape.111 = f32[640,4096]{1,0:T(8,128)} reshape(f32[64,10,4096]{2,1,0:T(8,128)} %copy.39) | data formatting | bytes 20971520 | tf_op jit(solution)/shard_map/convert_element_type | solution.py:68
  159.7 35.0 %all-gather.4.cloned.1.call-done = bf16[64,10,4096]{2,0,1:T(8,128)(2,1)} async-done(((bf16[16,10,4096]{2,0,1:T(8,128)(2,1)}), bf16[64,10,4096]{2,0,1:T(8,128)(2,1)}) %all-gather.4.cloned.1.call-update) | async-done | bytes 5242896 | tf_op jit(solution)/shard_map/all_gather | solution.py:55
  194.7 8.9 %copy.37 = bf16[64,10,4096]{2,1,0:T(8,128)(2,1)} copy(bf16[64,10,4096]{2,0,1:T(8,128)(2,1)} %all-gather.4.cloned.1.call-done) | data formatting | bytes 10485760 | tf_op jit(solution)/shard_map/all_gather | solution.py:55
  203.7 8.7 %reshape.105 = bf16[640,4096]{1,0:T(8,128)(2,1)} reshape(bf16[64,10,4096]{2,1,0:T(8,128)(2,1)} %copy.37) | data formatting | bytes 10485760 | tf_op jit(solution)/shard_map/reshape | solution.py:55
  217.0 4.6 multiply_convert_fusion.9
  224.2 21.3 %reduce-scatter.3.cloned.1.call-done = f32[1,16,10]{2,1,0:T(8,128)} async-done(((f32[4,16,10]{2,1,0:T(8,128)}), f32[1,16,10]{2,1,0:T(8,128)}) %reduce-scatter.3.cloned.1.call-update) | async-done | bytes 656 | tf_op jit(solution)/shard_map/reduce_scatter | solution.py:69
  245.5 9.9 %all-to-all-start.2 = ((f32[16,1,10]{2,1,0:T(1,128)}), f32[16,1,10]{2,1,0:T(1,128)S(1)}, u32[]{:S(2)}, u32[]{:S(2)}) async-start(f32[16,1,10]{2,1,0:T(1,128)} %bitcast.68), calls=%async_computation.3 | async-start | bytes 16384 | tf_op jit(solution)/shard_map/all_to_all | solution.py:72
  255.7 6.7 %all-to-all-done.2 = f32[16,1,10]{2,1,0:T(1,128)S(1)} async-done(((f32[16,1,10]{2,1,0:T(1,128)}), f32[16,1,10]{2,1,0:T(1,128)S(1)}, u32[]{:S(2)}, u32[]{:S(2)}) %all-to-all-start.2) | async-done | bytes 672 | tf_op jit(solution)/shard_map/all_to_all | solution.py:72
  264.0 10.1 %all_to_all.35 = bf16[16,1,10]{2,1,0:T(2,128)(2,1)S(1)} all-to-all(bf16[16,1,10]{2,1,0:T(2,128)(2,1)S(1)} %convert_element_type.125), channel_id=1, replica_groups=mesh['pipe'=4,'expert'=16,'dp'=4] {'expert'}, dimensions={0} | all-to-all | bytes 640 | tf_op jit(solution)/shard_map/all_to_all | solution.py:54
  274.1 9.0 %all-gather = bf16[64,1,10]{2,0,1:T(8,128)(2,1)S(1)} all-gather(bf16[16,1,10]{2,0,1:T(8,128)(2,1)S(1)} %copy.42), channel_id=2, replica_groups=mesh['pipe'=4,'expert'=16,'dp'=4] {'dp'}, dimensions={0}, use_global_device_ids=true | all-gather | bytes 1600 | tf_op jit(solution)/shard_map/all_gather | solution.py:57
  287.7 6.4 %copy.44 = bf16[64,10,4096]{2,1,0:T(8,128)(2,1)} copy(bf16[64,10,4096]{2,0,1:T(8,128)(2,1)S(1)} %multiply_convert_fusion.1) | data formatting | bytes 10485760 | tf_op jit(solution)/shard_map/convert_element_type | solution.py:58
  294.1 8.7 %convert_element_type.110 = bf16[640,4096]{1,0:T(8,128)(2,1)} reshape(bf16[64,10,4096]{2,1,0:T(8,128)(2,1)} %copy.44) | data formatting | bytes 10485760 | tf_op jit(solution)/shard_map/convert_element_type | solution.py:58
  302.8 5.0 %multiply_convert_fusion.7 = (bf16[640,192]{0,1:T(8,128)(2,1)S(1)}, bf16[640,192]{0,1:T(8,128)(2,1)S(1)}) fusion(f32[640,192]{0,1:T(8,128)S(1)} %copy-done.8, f32[640,192]{0,1:T(8,128)S(1)} %get-tuple-element.10, bf16[640,4096]{1,0:T(8,128)(2,1)} %convert_element_type.110, bf16[1,1,192,4096]{3,2,1,0:T(8,128)(2,1)} %param.13), kind=kOutput, calls=%fused_computation.27 | convolution fusion | flops 1008230400 | bytes 8290304 | tf_op jit(solution)/shard_map/dot_general | solution.py:76
  313.5 8.2 %reshape.108 = bf16[4,16,10,4096]{3,2,1,0:T(8,128)(2,1)} reshape(bf16[640,4096]{1,0:T(8,128)(2,1)} %add_convert_fusion) | data formatting | bytes 10485760 | tf_op jit(solution)/shard_map/reshape | solution.py:94
  321.7 80.8 %reduce-scatter.5.cloned.1.call-done = bf16[1,16,10,4096]{3,2,1,0:T(8,128)(2,1)} async-done(((bf16[4,16,10,4096]{3,2,1,0:T(8,128)(2,1)}), bf16[1,16,10,4096]{3,2,1,0:T(8,128)(2,1)}) %reduce-scatter.5.cloned.1.call-update) | async-done | bytes 1310736 | tf_op jit(solution)/shard_map/reduce_scatter | solution.py:95
  402.5 7.6 %all-to-all-start.4 = ((bf16[16,10,4096]{2,1,0:T(8,128)(2,1)}), bf16[16,10,4096]{2,1,0:T(8,128)(2,1)}, u32[]{:S(2)}, u32[]{:S(2)}) async-start(bf16[16,10,4096]{2,1,0:T(8,128)(2,1)} %bitcast.66), calls=%async_computation.6 | async-start | bytes 4194304 | tf_op jit(solution)/shard_map/all_to_all | solution.py:97
  410.8 48.4 %all-to-all-done.4 = bf16[16,10,4096]{2,1,0:T(8,128)(2,1)} async-done(((bf16[16,10,4096]{2,1,0:T(8,128)(2,1)}), bf16[16,10,4096]{2,1,0:T(8,128)(2,1)}, u32[]{:S(2)}, u32[]{:S(2)}) %all-to-all-start.4) | async-done | bytes 1310752 | tf_op jit(solution)/shard_map/all_to_all | solution.py:97
  464.1 5.0 %fusion.4 = bf16[1,1,192,4096]{3,2,1,0:T(8,128)(2,1)} fusion(bf16[640,192]{0,1:T(8,128)(2,1)S(1)} %get-tuple-element.8, bf16[640,4096]{1,0:T(8,128)(2,1)} %reshape.105), kind=kOutput, calls=%fused_computation.13 | convolution fusion | flops 1007419392 | bytes 7061504 | tf_op jit(solution)/shard_map/dot_general | solution.py:86
  469.3 5.0 %fusion.5 = bf16[1,1,192,4096]{3,2,1,0:T(8,128)(2,1)} fusion(bf16[640,192]{0,1:T(8,128)(2,1)S(1)} %copy-done.2, bf16[640,4096]{1,0:T(8,128)(2,1)} %reshape.105), kind=kOutput, calls=%fused_computation.14 | convolution fusion | flops 1007419392 | bytes 7061504 | tf_op jit(solution)/shard_map/dot_general | solution.py:89
  474.3 6.6 %fusion.3 = bf16[1,1,192,4096]{3,2,1,0:T(8,128)(2,1)} fusion(bf16[640,192]{0,1:T(8,128)(2,1)S(1)} %get-tuple-element.9, f32[640,4096]{1,0:T(8,128)} %reshape.111, f32[640]{0:T(1024)S(1)} %reshape.112), kind=kOutput, calls=%fused_computation.12 | convolution fusion | flops 1012662272 | bytes 12306944 | tf_op jit(solution)/shard_map/dot_general | solution.py:83
  480.9 8.2 %collective-permute-done = bf16[128,4096]{1,0:T(8,128)(2,1)S(1)} collective-permute-done((bf16[128,4096]{1,0:T(8,128)(2,1)}, bf16[128,4096]{1,0:T(8,128)(2,1)S(1)}, u32[]{:S(2)}, u32[]{:S(2)}) %collective-permute-start) | collective-permute-done | bytes 1048608 | tf_op jit(solution)/shard_map/ppermute | solution.py:10
  (70 shorter events, 38.9 us)
Async XLA Ops:
  7.2 209.8 %copy-start = (bf16[1,1,192,4096]{3,2,1,0:T(8,128)(2,1)S(1)}, bf16[1,1,192,4096]{3,2,1,0:T(8,128)(2,1)}, u32[]{:S(2)}) copy-start(bf16[1,1,192,4096]{3,2,1,0:T(8,128)(2,1)} %param.12) | copy-start | bytes 4718596
  7.2 128.0 %all-gather.6.cloned.1.call-start = ((), (), s32[]{:S(2)}) async-start(), calls=%async_computation.8 | async-start | bytes 6553600 | tf_op jit(solution)/shard_map/all_gather | solution.py:56
  75.9 118.9 %all-gather.4.cloned.1.call-start = ((), (), s32[]{:S(2)}) async-start(), calls=%async_computation.7 | async-start | bytes 6553600 | tf_op jit(solution)/shard_map/all_gather | solution.py:55
  133.1 2.0 copy-start.6
  134.9 110.6 %reduce-scatter.3.cloned.1.call-start = ((), (), s32[]{:S(2)}) async-start(), calls=%async_computation.9 | async-start | bytes 40960 | tf_op jit(solution)/shard_map/reduce_scatter | solution.py:69
  203.7 8.7 %copy-start.4 = (bf16[1,1,192,4096]{3,2,1,0:T(8,128)(2,1)S(1)}, bf16[1,1,192,4096]{3,2,1,0:T(8,128)(2,1)}, u32[]{:S(2)}) copy-start(bf16[1,1,192,4096]{3,2,1,0:T(8,128)(2,1)} %param.11) | copy-start | bytes 4718596
  212.4 9.2 %slice-start = ((s8[10485760]{0:T(1024)(128)(4,1)}), s8[4194304]{0:T(1024)(128)(4,1)S(1)}, s32[]{:S(2)}) async-start(s8[10485760]{0:T(1024)(128)(4,1)} %bitcast.64), calls=%async_computation.11 | async-start | bytes 8388608
  212.4 9.2 %slice-start.1 = ((s8[10485760]{0:T(1024)(128)(4,1)}), s8[4194304]{0:T(1024)(128)(4,1)S(1)}, s32[]{:S(2)}) async-start(s8[10485760]{0:T(1024)(128)(4,1)} %bitcast.64), calls=%async_computation.12 | async-start | bytes 8388608
  216.9 4.6 copy-start.7
  216.9 4.6 slice-start.2
  216.9 4.6 copy-start.3
  245.5 16.9 %all-to-all-start.2 = ((f32[16,1,10]{2,1,0:T(1,128)}), f32[16,1,10]{2,1,0:T(1,128)S(1)}, u32[]{:S(2)}, u32[]{:S(2)}) async-start(f32[16,1,10]{2,1,0:T(1,128)} %bitcast.68), calls=%async_computation.3 | async-start | bytes 16384 | tf_op jit(solution)/shard_map/all_to_all | solution.py:72
  255.4 147.1 %reduce-scatter.5.cloned.1.call-start = ((), (), s32[]{:S(2)}) async-start(), calls=%async_computation.10 | async-start | bytes 10485760 | tf_op jit(solution)/shard_map/reduce_scatter | solution.py:95
  294.1 8.7 %copy-start.8 = (f32[640,192]{0,1:T(8,128)S(1)}, f32[640,192]{0,1:T(8,128)}, u32[]{:S(2)}) copy-start(f32[640,192]{0,1:T(8,128)} %copy-done.7) | copy-start | bytes 1474564
  302.8 5.0 %copy-start.5 = (bf16[1,1,192,4096]{3,2,1,0:T(8,128)(2,1)S(1)}, bf16[1,1,192,4096]{3,2,1,0:T(8,128)(2,1)}, u32[]{:S(2)}) copy-start(bf16[1,1,192,4096]{3,2,1,0:T(8,128)(2,1)} %param.11) | copy-start | bytes 4718596
  307.8 1.6 copy-start.1
  402.5 56.7 %all-to-all-start.4 = ((bf16[16,10,4096]{2,1,0:T(8,128)(2,1)}), bf16[16,10,4096]{2,1,0:T(8,128)(2,1)}, u32[]{:S(2)}, u32[]{:S(2)}) async-start(bf16[16,10,4096]{2,1,0:T(8,128)(2,1)} %bitcast.66), calls=%async_computation.6 | async-start | bytes 4194304 | tf_op jit(solution)/shard_map/all_to_all | solution.py:97
  462.4 6.9 %copy-start.2 = (bf16[640,192]{0,1:T(8,128)(2,1)S(1)}, bf16[640,192]{0,1:T(8,128)(2,1)}, u32[]{:S(2)}) copy-start(bf16[640,192]{0,1:T(8,128)(2,1)} %copy-done.1) | copy-start | bytes 737284
  462.4 26.6 %collective-permute-start = (bf16[128,4096]{1,0:T(8,128)(2,1)}, bf16[128,4096]{1,0:T(8,128)(2,1)S(1)}, u32[]{:S(2)}, u32[]{:S(2)}) collective-permute-start(bf16[128,4096]{1,0:T(8,128)(2,1)} %convolution_convert_fusion.4), channel_id=1, source_target_pairs={{64,0},{128,64},{192,128},{65,1},{129,65},{193,129},{66,2},{130,66... | collective-permute-start | bytes 3145736 | tf_op jit(solution)/shard_map/ppermute | solution.py:10
Sparse Core Ops, SparseCore 0:
  76.0 56.2 all-gather.5
  135.1 59.6 all-gather.3
  224.3 21.1 reduce-scatter.2
  321.8 80.6 reduce-scatter.4
where the time goes:
time: 498 us; the launch traced here: 497 us
  waiting for transfers between devices  200 us (40%)
  blocking collectives  134 us (27%)
  local copies, waits for them, and re-layouts  76.7 us (15%)
  matrix products  43 us (9%)
  starting transfers between devices  19.8 us (4%)
  between operations  14.1 us (3%)
  other arithmetic  8.57 us (2%)
    reduce_scatter x1, waiting for transfers between devices, per_device(): summed = lax.psum_scatter(outgoing, 'dp', scatter_dimension=0, tiled=True)  80.8 us
    all_to_all x1, blocking collectives, per_device(): up_e = lax.all_to_all(local_up, 'expert', 0, 0, tiled=True)  61 us
    all_to_all x1, blocking collectives, per_device(): x_e = lax.all_to_all(local_x, 'expert', 0, 0, tiled=True)  53.9 us
    all_to_all x1, waiting for transfers between devices, per_device(): lax.all_to_all(summed, 'expert', 0, 0, tiled=True).reshape(-1, model_width)  48.4 us
    all_gather x1, waiting for transfers between devices, per_device(): lax.all_gather(x_e, 'dp', axis=0, tiled=True).reshape(-1, model_width)  35 us
    convert_element_type x2, local copies, waits for them, and re-layouts, per_device(): row_score = jnp.sum(partial_out * rows_up.astype(jnp.float32), axis=1)  24.5 us
    reduce_scatter x1, waiting for transfers between devices, per_device(): lax.psum_scatter(row_score.reshape(groups, experts, capacity), 'dp', scat...  21.3 us
    convert_element_type x2, local copies, waits for them, and re-layouts, per_device(): (rows_gate.astype(jnp.float32)[:, None] * rows_up.astype(jnp.float32)).as...  15.1 us
  transfers between devices with their start and end apart: 7, of which 6 were waited for; matrix products, arithmetic and copies ran while one was open for 9% of the time, Pallas kernels for 0%

commit v1 on v0

--- a/solution.py
+++ b/solution.py
@@ -52,7 +52,9 @@
     x_e = lax.all_to_all(local_x, "expert", 0, 0, tiled=True)
     up_e = lax.all_to_all(local_up, "expert", 0, 0, tiled=True)
     gate_e = lax.all_to_all(local_gate, "expert", 0, 0, tiled=True)
-    rows_x = lax.all_gather(x_e, "dp", axis=0, tiled=True).reshape(-1, model_width)
+    rows_x = jnp.concatenate(
+        lax.all_to_all(jnp.stack([x_e] * lax.axis_size("dp")), "dp", 0, 0), axis=0
+    ).reshape(-1, model_width)
     rows_up = lax.all_gather(up_e, "dp", axis=0, tiled=True).reshape(-1, model_width)
     rows_gate = lax.all_gather(gate_e, "dp", axis=0, tiled=True).reshape(-1)
     rows_grad = (rows_gate.astype(jnp.float32)[:, None] * rows_up.astype(jnp.float32)).astype(

time: 498 us -> 526 us (1.056)
  waiting for transfers between devices: 200 us -> 220 us
    all_to_all x0 -> x1, waiting for transfers between devices: none -> 59.5 us  [per_device(): lax.all_to_all(jnp.stack([x_e] * lax.axis_size('dp')), 'dp', 0, 0)]
    all_gather x1 -> x0, waiting for transfers between devices: 35 us -> none  [per_device(): lax.all_gather(x_e, 'dp', axis=0, tiled=True).reshape(-1, model_width)]
    another operation x0 -> x2, local copies, waits for them, and re-layouts: none -> 11.7 us  [the longest x1 8.78 us: per_device(): rows_x = jnp.concatenate(lax.all_to_all(jnp.stack([x_e] * lax.axis_size('...]
    all_to_all x0 -> x1, local copies, waits for them, and re-layouts: none -> 9.1 us  [per_device(): lax.all_to_all(jnp.stack([x_e] * lax.axis_size('dp')), 'dp', 0, 0)]
    all_gather x1 -> x0, local copies, waits for them, and re-layouts: 8.94 us -> none  [per_device(): lax.all_gather(x_e, 'dp', axis=0, tiled=True).reshape(-1, model_width)]
    reshape x1 -> x0, local copies, waits for them, and re-layouts: 8.72 us -> none  [per_device(): lax.all_gather(x_e, 'dp', axis=0, tiled=True).reshape(-1, model_width)]
where the time goes in v1:
time: 526 us; the launch traced here: 525 us
  waiting for transfers between devices  220 us (42%)
  blocking collectives  134 us (25%)
  local copies, waits for them, and re-layouts  78.7 us (15%)
  matrix products  44.6 us (8%)
  starting transfers between devices  25 us (5%)
  between operations  14 us (3%)
  other arithmetic  8.57 us (2%)
    reduce_scatter x1, waiting for transfers between devices, per_device(): summed = lax.psum_scatter(outgoing, 'dp', scatter_dimension=0, tiled=True)  80.8 us
    all_to_all x1, blocking collectives, per_device(): up_e = lax.all_to_all(local_up, 'expert', 0, 0, tiled=True)  61 us
    all_to_all x1, waiting for transfers between devices, per_device(): lax.all_to_all(jnp.stack([x_e] * lax.axis_size('dp')), 'dp', 0, 0)  59.5 us
    all_to_all x1, blocking collectives, per_device(): x_e = lax.all_to_all(local_x, 'expert', 0, 0, tiled=True)  53.9 us
    all_to_all x1, waiting for transfers between devices, per_device(): lax.all_to_all(summed, 'expert', 0, 0, tiled=True).reshape(-1, model_width)  48.4 us
    convert_element_type x2, local copies, waits for them, and re-layouts, per_device(): row_score = jnp.sum(partial_out * rows_up.astype(jnp.float32), axis=1)  23.7 us
    reduce_scatter x1, waiting for transfers between devices, per_device(): lax.psum_scatter(row_score.reshape(groups, experts, capacity), 'dp', scat...  16.4 us
    convert_element_type x2, local copies, waits for them, and re-layouts, per_device(): (rows_gate.astype(jnp.float32)[:, None] * rows_up.astype(jnp.float32)).as...  15.1 us
  transfers between devices with their start and end apart: 7, of which 6 were waited for; matrix products, arithmetic and copies ran while one was open for 9% of the time, Pallas kernels for 0%

profile of v1, /device:TPU:1, one launch (start us, length us, event | category | flops | bytes accessed | tf_op | source)
XLA Modules:
  0.0 525.0 jit_solution(10714696820215009246)
XLA Ops:
  13.1 61.0 %all_to_all.38 = bf16[16,10,4096]{2,1,0:T(8,128)(2,1)S(1)} all-to-all(bf16[16,10,4096]{2,1,0:T(8,128)(2,1)} %reshape.104), channel_id=1, replica_groups=mesh['pipe'=4,'expert'=16,'dp'=4] {'expert'}, dimensions={0} | all-to-all | bytes 2621440 | tf_op jit(solution)/shard_map/all_to_all | solution.py:53
  79.2 53.9 %all_to_all.39 = bf16[16,10,4096]{2,1,0:T(8,128)(2,1)S(1)} all-to-all(bf16[16,10,4096]{2,1,0:T(8,128)(2,1)} %reshape.103), channel_id=1, replica_groups=mesh['pipe'=4,'expert'=16,'dp'=4] {'expert'}, dimensions={0} | all-to-all | bytes 2621440 | tf_op jit(solution)/shard_map/all_to_all | solution.py:52
  136.7 5.2 all-to-all-start.1
  142.3 59.5 %all-to-all-done.1 = bf16[4,16,10,4096]{3,1,2,0:T(8,128)(2,1)} async-done(((bf16[4,16,10,4096]{3,1,2,0:T(8,128)(2,1)}), bf16[4,16,10,4096]{3,1,2,0:T(8,128)(2,1)}, u32[]{:S(2)}, u32[]{:S(2)}) %all-to-all-start.1) | async-done | bytes 5242912 | tf_op jit(solution)/shard_map/all_to_all | solution.py:56
  201.8 9.1 %copy.37 = bf16[4,16,10,4096]{3,2,1,0:T(8,128)(2,1)} copy(bf16[4,16,10,4096]{3,1,2,0:T(8,128)(2,1)} %all-to-all-done.1) | data formatting | bytes 10485760 | tf_op jit(solution)/shard_map/all_to_all | solution.py:56
  210.9 8.8 %reshape_reshape.3 = bf16[640,4096]{1,0:T(8,128)(2,1)} reshape(bf16[4,16,10,4096]{3,2,1,0:T(8,128)(2,1)} %copy.37) | data formatting | bytes 10485760 | tf_op jit(solution)/shard_map/reshape;reshape | solution.py:57
  226.9 11.9 %copy.39 = f32[64,10,4096]{2,1,0:T(8,128)} copy(bf16[64,10,4096]{2,0,1:T(8,128)(2,1)} %all-gather.3.cloned.1.call-done) | data formatting | bytes 15728640 | tf_op jit(solution)/shard_map/convert_element_type | solution.py:70
  238.7 11.9 %reshape.109 = f32[640,4096]{1,0:T(8,128)} reshape(f32[64,10,4096]{2,1,0:T(8,128)} %copy.39) | data formatting | bytes 20971520 | tf_op jit(solution)/shard_map/convert_element_type | solution.py:70
  250.6 6.1 %multiply_reduce_fusion = f32[640]{0:T(1024)S(1)} fusion(f32[640,4096]{1,0:T(8,128)} %reshape.109, bf16[640,192]{0,1:T(8,128)(2,1)S(1)} %get-tuple-element.9, bf16[1,1,192,4096]{3,2,1,0:T(8,128)(2,1)} %param.13), kind=kOutput, calls=%fused_computation.3 | convolution fusion | flops 1011875200 | bytes 12306944 | tf_op jit(solution)/shard_map/dot_general | solution.py:69
  257.5 16.4 %reduce-scatter.3.cloned.1.call-done = f32[1,16,10]{2,1,0:T(8,128)} async-done(((f32[4,16,10]{2,1,0:T(8,128)}), f32[1,16,10]{2,1,0:T(8,128)}) %reduce-scatter.3.cloned.1.call-update) | async-done | bytes 656 | tf_op jit(solution)/shard_map/reduce_scatter | solution.py:71
  273.9 9.9 %all-to-all-start.3 = ((f32[16,1,10]{2,1,0:T(1,128)}), f32[16,1,10]{2,1,0:T(1,128)S(1)}, u32[]{:S(2)}, u32[]{:S(2)}) async-start(f32[16,1,10]{2,1,0:T(1,128)} %bitcast.66), calls=%async_computation.4 | async-start | bytes 16384 | tf_op jit(solution)/shard_map/all_to_all | solution.py:74
  284.1 6.7 %all-to-all-done.3 = f32[16,1,10]{2,1,0:T(1,128)S(1)} async-done(((f32[16,1,10]{2,1,0:T(1,128)}), f32[16,1,10]{2,1,0:T(1,128)S(1)}, u32[]{:S(2)}, u32[]{:S(2)}) %all-to-all-start.3) | async-done | bytes 672 | tf_op jit(solution)/shard_map/all_to_all | solution.py:74
  292.4 10.1 %all_to_all.40 = bf16[16,1,10]{2,1,0:T(2,128)(2,1)S(1)} all-to-all(bf16[16,1,10]{2,1,0:T(2,128)(2,1)S(1)} %convert_element_type.125), channel_id=1, replica_groups=mesh['pipe'=4,'expert'=16,'dp'=4] {'expert'}, dimensions={0} | all-to-all | bytes 640 | tf_op jit(solution)/shard_map/all_to_all | solution.py:54
  302.5 9.0 %all-gather = bf16[64,1,10]{2,0,1:T(8,128)(2,1)S(1)} all-gather(bf16[16,1,10]{2,0,1:T(8,128)(2,1)S(1)} %copy.42), channel_id=2, replica_groups=mesh['pipe'=4,'expert'=16,'dp'=4] {'dp'}, dimensions={0}, use_global_device_ids=true | all-gather | bytes 1600 | tf_op jit(solution)/shard_map/all_gather | solution.py:59
  316.1 6.4 %copy.44 = bf16[64,10,4096]{2,1,0:T(8,128)(2,1)} copy(bf16[64,10,4096]{2,0,1:T(8,128)(2,1)S(1)} %multiply_convert_fusion.1) | data formatting | bytes 10485760 | tf_op jit(solution)/shard_map/convert_element_type | solution.py:60
  322.6 8.6 %convert_element_type.110 = bf16[640,4096]{1,0:T(8,128)(2,1)} reshape(bf16[64,10,4096]{2,1,0:T(8,128)(2,1)} %copy.44) | data formatting | bytes 10485760 | tf_op jit(solution)/shard_map/convert_element_type | solution.py:60
  341.9 8.2 %reshape.106 = bf16[4,16,10,4096]{3,2,1,0:T(8,128)(2,1)} reshape(bf16[640,4096]{1,0:T(8,128)(2,1)} %add_convert_fusion) | data formatting | bytes 10485760 | tf_op jit(solution)/shard_map/reshape | solution.py:96
  350.1 80.8 %reduce-scatter.5.cloned.1.call-done = bf16[1,16,10,4096]{3,2,1,0:T(8,128)(2,1)} async-done(((bf16[4,16,10,4096]{3,2,1,0:T(8,128)(2,1)}), bf16[1,16,10,4096]{3,2,1,0:T(8,128)(2,1)}) %reduce-scatter.5.cloned.1.call-update) | async-done | bytes 1310736 | tf_op jit(solution)/shard_map/reduce_scatter | solution.py:97
  430.9 7.6 %all-to-all-start.5 = ((bf16[16,10,4096]{2,1,0:T(8,128)(2,1)}), bf16[16,10,4096]{2,1,0:T(8,128)(2,1)}, u32[]{:S(2)}, u32[]{:S(2)}) async-start(bf16[16,10,4096]{2,1,0:T(8,128)(2,1)} %bitcast.64), calls=%async_computation.7 | async-start | bytes 4194304 | tf_op jit(solution)/shard_map/all_to_all | solution.py:99
  439.2 48.4 %all-to-all-done.5 = bf16[16,10,4096]{2,1,0:T(8,128)(2,1)} async-done(((bf16[16,10,4096]{2,1,0:T(8,128)(2,1)}), bf16[16,10,4096]{2,1,0:T(8,128)(2,1)}, u32[]{:S(2)}, u32[]{:S(2)}) %all-to-all-start.5) | async-done | bytes 1310752 | tf_op jit(solution)/shard_map/all_to_all | solution.py:99
  492.5 5.0 fusion.4
  497.7 5.0 fusion.5
  502.7 6.6 %fusion.3 = bf16[1,1,192,4096]{3,2,1,0:T(8,128)(2,1)} fusion(bf16[640,192]{0,1:T(8,128)(2,1)S(1)} %get-tuple-element.9, f32[640,4096]{1,0:T(8,128)} %reshape.109, f32[640]{0:T(1024)S(1)} %reshape.110), kind=kOutput, calls=%fused_computation.12 | convolution fusion | flops 1012662272 | bytes 12306944 | tf_op jit(solution)/shard_map/dot_general | solution.py:85
  509.3 8.2 %collective-permute-done = bf16[128,4096]{1,0:T(8,128)(2,1)S(1)} collective-permute-done((bf16[128,4096]{1,0:T(8,128)(2,1)}, bf16[128,4096]{1,0:T(8,128)(2,1)S(1)}, u32[]{:S(2)}, u32[]{:S(2)}) %collective-permute-start) | collective-permute-done | bytes 1048608 | tf_op jit(solution)/shard_map/ppermute | solution.py:10
  (63 shorter events, 46.5 us)
Async XLA Ops:
  7.2 217.8 %copy-start = (bf16[1,1,192,4096]{3,2,1,0:T(8,128)(2,1)S(1)}, bf16[1,1,192,4096]{3,2,1,0:T(8,128)(2,1)}, u32[]{:S(2)}) copy-start(bf16[1,1,192,4096]{3,2,1,0:T(8,128)(2,1)} %param.12) | copy-start | bytes 4718596
  7.2 219.7 %all-gather.3.cloned.1.call-start = ((), (), s32[]{:S(2)}) async-start(), calls=%async_computation.8 | async-start | bytes 6553600 | tf_op jit(solution)/shard_map/all_gather | solution.py:58
  136.7 5.5 %copy-start.6 = (f32[1,128,8]{1,2,0:T(8,128)S(1)}, f32[1,128,8]{1,2,0:T(8,128)}, u32[]{:S(2)}) copy-start(f32[1,128,8]{1,2,0:T(8,128)} %param.9) | copy-start | bytes 12292
  136.7 65.0 %all-to-all-start.1 = ((bf16[4,16,10,4096]{3,1,2,0:T(8,128)(2,1)}), bf16[4,16,10,4096]{3,1,2,0:T(8,128)(2,1)}, u32[]{:S(2)}, u32[]{:S(2)}) async-start(bf16[4,16,10,4096]{3,1,2,0:T(8,128)(2,1)} %stack.2), calls=%async_computation.1 | async-start | bytes 10485760 | tf_op jit(solution)/shard_map/all_to_all | solution.py:56
  142.0 131.9 %reduce-scatter.3.cloned.1.call-start = ((), (), s32[]{:S(2)}) async-start(), calls=%async_computation.9 | async-start | bytes 40960 | tf_op jit(solution)/shard_map/reduce_scatter | solution.py:71
  210.9 8.8 %copy-start.4 = (bf16[1,1,192,4096]{3,2,1,0:T(8,128)(2,1)S(1)}, bf16[1,1,192,4096]{3,2,1,0:T(8,128)(2,1)}, u32[]{:S(2)}) copy-start(bf16[1,1,192,4096]{3,2,1,0:T(8,128)(2,1)} %param.11) | copy-start | bytes 4718596
  219.6 5.3 %copy-start.1 = (bf16[640,4096]{1,0:T(8,128)(2,1)S(1)}, bf16[640,4096]{1,0:T(8,128)(2,1)}, u32[]{:S(2)}) copy-start(bf16[640,4096]{1,0:T(8,128)(2,1)} %reshape_reshape.3) | copy-start | bytes 15728644
  224.2 0.8 copy-start.7
  273.9 16.9 %all-to-all-start.3 = ((f32[16,1,10]{2,1,0:T(1,128)}), f32[16,1,10]{2,1,0:T(1,128)S(1)}, u32[]{:S(2)}, u32[]{:S(2)}) async-start(f32[16,1,10]{2,1,0:T(1,128)} %bitcast.66), calls=%async_computation.4 | async-start | bytes 16384 | tf_op jit(solution)/shard_map/all_to_all | solution.py:74
  283.8 147.0 %reduce-scatter.5.cloned.1.call-start = ((), (), s32[]{:S(2)}) async-start(), calls=%async_computation.10 | async-start | bytes 10485760 | tf_op jit(solution)/shard_map/reduce_scatter | solution.py:97
  322.6 8.6 %copy-start.8 = (f32[640,192]{0,1:T(8,128)S(1)}, f32[640,192]{0,1:T(8,128)}, u32[]{:S(2)}) copy-start(f32[640,192]{0,1:T(8,128)} %copy-done.7) | copy-start | bytes 1474564
  331.2 5.0 copy-start.5
  336.2 1.6 copy-start.2
  430.9 56.7 %all-to-all-start.5 = ((bf16[16,10,4096]{2,1,0:T(8,128)(2,1)}), bf16[16,10,4096]{2,1,0:T(8,128)(2,1)}, u32[]{:S(2)}, u32[]{:S(2)}) async-start(bf16[16,10,4096]{2,1,0:T(8,128)(2,1)} %bitcast.64), calls=%async_computation.7 | async-start | bytes 4194304 | tf_op jit(solution)/shard_map/all_to_all | solution.py:99
  490.8 6.9 %copy-start.3 = (bf16[640,192]{0,1:T(8,128)(2,1)S(1)}, bf16[640,192]{0,1:T(8,128)(2,1)}, u32[]{:S(2)}) copy-start(bf16[640,192]{0,1:T(8,128)(2,1)} %copy-done.2) | copy-start | bytes 737284
  490.8 26.6 %collective-permute-start = (bf16[128,4096]{1,0:T(8,128)(2,1)}, bf16[128,4096]{1,0:T(8,128)(2,1)S(1)}, u32[]{:S(2)}, u32[]{:S(2)}) collective-permute-start(bf16[128,4096]{1,0:T(8,128)(2,1)} %convolution_convert_fusion.4), channel_id=1, source_target_pairs={{64,0},{128,64},{192,128},{65,1},{129,65},{193,129},{66,2},{130,66... | collective-permute-start | bytes 3145736 | tf_op jit(solution)/shard_map/ppermute | solution.py:10
Sparse Core Ops, SparseCore 0:
  76.0 56.2 all-gather.2
  257.6 16.2 reduce-scatter.2
  350.2 80.6 reduce-scatter.4
